TPU v7x, 32 devices: a whole 2x2x4 slice. The times are simulated.
32 devices in a mesh: grp: 2 (over y), blk: 8 (over z, x), bin: 2 (over core).
Axes of the slice: x: 2, y: 2, z: 4, core: 2. Of those that a mesh axis runs over, the one named last changes fastest.
Arguments:
- units: bfloat16 [1024, 32768], P(('grp', 'bin'), 'blk'), parts along dimension 0, may hold values from -6 to 6
- cotangent: bfloat16 [1024, 32768], P(('grp', 'bin'), 'blk'), parts along dimension 0, may hold values from -6 to 6
- left_factor: bfloat16 [64, 512, 512], P('blk', 'bin'), may hold values from -0.25 to 0.25
- right_factor: bfloat16 [512, 64, 64], P('blk', 'bin'), may hold values from -0.75 to 0.75
- session_units: int32 [128], P(('grp', 'blk')), parts along dimension 0, may hold values from 128 to 512, as said below
Outputs:
- grad_left: bfloat16 [128, 512, 512], P(('grp', 'blk'), 'bin'), parts along dimension 0
- grad_right: bfloat16 [1024, 64, 64], P(('grp', 'blk'), 'bin'), parts along dimension 0
There are 2 independent parts, one for each index of `grp`. A program takes and returns all parts, laid end to end along the dimension named above; an argument that names none is the same for every part. Nothing has to cross between parts.
Inputs may be any that keep to these rules, and one draw needn't show every extreme that they name: `session_units`: each count is a multiple of a quarter of 512; some session of every group has all 512 units live.
All inputs are finite; a program needn't handle non-finite values.
Results may differ from a plain program's by a relative error of at most 0.0049.
Values may be sent and summed in bfloat16 or wider, within the bound.
No kernel may reach another device: no remote copies, remote signals or barrier semaphores. Data moves between devices by JAX's collectives and lax.ppermute only.
A program may use at most 128 MiB of HBM per device.

v0:
```python
import jax
import jax.numpy as jnp
from jax import lax
from jax.sharding import PartitionSpec as P


def on_device(units, cotangent, left_factor, right_factor, session_units):
    row_count = units.shape[0]
    local_blocks = left_factor.shape[0]
    block_size = left_factor.shape[2]
    right_local = right_factor.shape[0]
    order_right = right_factor.shape[2]
    peer_count = lax.axis_size("blk")
    unit_mask = (jnp.arange(block_size)[None, :] < session_units[:, None]).astype(jnp.bfloat16)
    inputs = units.reshape(row_count, local_blocks, block_size) * unit_mask[None]
    left_full = lax.all_gather(left_factor, "bin", axis=1, tiled=True)
    mixed = jnp.einsum(
        "rki,kij->kjr", inputs, left_full, preferred_element_type=jnp.float32
    ).astype(jnp.bfloat16)
    mixed_sent = mixed.reshape(local_blocks, peer_count, right_local, row_count)
    mixed_got = lax.all_to_all(mixed_sent, "blk", split_axis=1, concat_axis=0, tiled=True)
    permuted = mixed_got.reshape(order_right, right_local, row_count)
    upstream = cotangent.reshape(row_count, right_local, order_right)
    right_full = lax.all_gather(right_factor, "bin", axis=1, tiled=True)
    back_grad = jnp.einsum(
        "rjm,jkm->jkr", upstream, right_full, preferred_element_type=jnp.float32
    ).astype(jnp.bfloat16)
    back_sent = back_grad.reshape(right_local, peer_count, local_blocks, row_count)
    back_got = lax.all_to_all(back_sent, "blk", split_axis=1, concat_axis=0, tiled=True)
    returned = back_got.reshape(block_size, local_blocks, row_count)
    right_term = jnp.einsum("kjr,rjm->jkm", permuted, upstream, preferred_element_type=jnp.float32)
    grad_right = lax.psum_scatter(right_term, "bin", scatter_dimension=1, tiled=True).astype(
        jnp.bfloat16
    )
    left_term = jnp.einsum("rki,jkr->kij", inputs, returned, preferred_element_type=jnp.float32)
    grad_left = lax.psum_scatter(left_term, "bin", scatter_dimension=1, tiled=True).astype(
        jnp.bfloat16
    )
    return (grad_left, grad_right)


def solution(mesh):
    placed = (
        P(("grp", "bin"), "blk"),
        P(("grp", "bin"), "blk"),
        P("blk", "bin", None),
        P("blk", "bin", None),
        P(("grp", "blk")),
    )
    return jax.shard_map(
        on_device,
        mesh=mesh,
        in_specs=placed,
        out_specs=(P(("grp", "blk"), "bin", None), P(("grp", "blk"), "bin", None)),
        check_vma=False,
    )
```

profile of v0, /device:TPU:0, one launch (start us, length us, event | category | flops | bytes accessed | tf_op | source)
XLA Modules:
  0.0 175.1 jit_solution(1585854343197089779)
XLA Ops:
  7.2 0.0 copy-start.3
  7.2 0.0 copy-start
  7.2 0.0 all-gather.2.cloned.1.call-start
  7.2 0.7 all-gather.2.cloned.1.call-update
  7.9 0.0 copy-done.3
  7.9 0.1 fusion.6
  8.0 18.0 %all-gather.2.cloned.1.call-done = bf16[8,512,512]{2,1,0:T(8,128)(2,1)} async-done(((bf16[8,256,512]{2,1,0:T(8,128)(2,1)}), bf16[8,512,512]{2,1,0:T(8,128)(2,1)}) %all-gather.2.cloned.1.call-update) | async-done | bytes 4194320 | tf_op jit(solution)/shard_map/all_gather | solution.py:16
  26.0 0.0 copy-done
  26.0 4.8 %convert_bitcast_fusion = bf16[8,512,256]{1,2,0:T(8,128)(2,1)} fusion(bf16[8,512,512]{2,1,0:T(8,128)(2,1)} %all-gather.2.cloned.1.call-done, bf16[32,8,8,512]{3,2,1,0:T(8,128)(2,1)S(1)} %bitcast.30, bf16[8,512]{1,0:T(8,128)(2,1)S(1)} %fusion.6), kind=kOutput, calls=%fused_computation.4 | convolution fusion | flops 1075838976 | bytes 8396800 | tf_op jit(solution)/shard_map/rki,kij->kjr/dot_general | solution.py:17
  30.7 2.8 %copy.24 = bf16[8,512,256]{2,1,0:T(8,128)(2,1)S(1)} copy(bf16[8,512,256]{1,2,0:T(8,128)(2,1)} %convert_bitcast_fusion) | data formatting | bytes 4194304 | tf_op jit(solution)/shard_map/convert_element_type | solution.py:19
  33.6 1.5 copy.25
  35.1 5.8 %all-to-all-start.1 = ((bf16[8,8,64,256]{3,2,0,1:T(8,128)(2,1)}), bf16[8,8,64,256]{3,2,0,1:T(8,128)(2,1)}, u32[]{:S(2)}, u32[]{:S(2)}) async-start(bf16[8,8,64,256]{3,2,0,1:T(8,128)(2,1)} %copy.25), calls=%async_computation.2 | async-start | bytes 4194304 | tf_op jit(solution)/shard_map/all_to_all | solution.py:21
  40.8 0.0 copy-start.2
  40.8 3.3 %copy.20 = bf16[256,4096]{0,1:T(8,128)(2,1)S(1)} copy(bf16[256,4096]{1,0:T(8,128)(2,1)} %param.6) | data formatting | bytes 4194304 | tf_op args[1]
  44.2 0.0 copy-done.2
  44.2 2.6 %all_gather.6 = bf16[64,64,64]{2,1,0:T(8,128)(2,1)S(1)} all-gather(bf16[64,32,64]{2,1,0:T(8,128)(2,1)S(1)} %copy-done.2), channel_id=1, replica_groups=mesh['grp'=2,'blk'=8,'bin'=2] {'bin'}, dimensions={1}, use_global_device_ids=true | all-gather | bytes 786432 | tf_op jit(solution)/shard_map/all_gather | solution.py:24
  46.7 0.7 convert_bitcast_fusion.1
  47.4 1.5 copy.21
  48.9 40.7 %all-to-all-done.1 = bf16[8,8,64,256]{3,2,0,1:T(8,128)(2,1)} async-done(((bf16[8,8,64,256]{3,2,0,1:T(8,128)(2,1)}), bf16[8,8,64,256]{3,2,0,1:T(8,128)(2,1)}, u32[]{:S(2)}, u32[]{:S(2)}) %all-to-all-start.1) | async-done | bytes 2097184 | tf_op jit(solution)/shard_map/all_to_all | solution.py:21
  89.6 4.4 %all-to-all-start = ((bf16[64,8,8,256]{3,2,0,1:T(8,128)(2,1)}), bf16[64,8,8,256]{3,2,0,1:T(8,128)(2,1)}, u32[]{:S(2)}, u32[]{:S(2)}) async-start(bf16[64,8,8,256]{3,2,0,1:T(8,128)(2,1)} %copy.21), calls=%async_computation | async-start | bytes 4194304 | tf_op jit(solution)/shard_map/all_to_all | solution.py:29
  94.0 0.0 reduce-scatter.5.cloned.1.call-start
  94.0 4.3 %fusion = f32[64,64,64]{2,1,0:T(8,128)} fusion(bf16[256,64,64]{0,2,1:T(8,128)(2,1)S(1)} %bitcast.27, bf16[8,8,1,64,256]{4,3,1,0,2:T(8,128)(2,1)} %bitcast.8), kind=kOutput, calls=%fused_computation.1 | convolution fusion | flops 134217728 | bytes 5242880 | tf_op jit(solution)/shard_map/kjr,rjm->jkm/dot_general | solution.py:31
  98.3 0.0 reduce-scatter.5.cloned.1.call-update
  98.4 0.0 reduce-scatter.3.cloned.1.call-start
  98.4 43.4 %all-to-all-done = bf16[64,8,8,256]{3,2,0,1:T(8,128)(2,1)} async-done(((bf16[64,8,8,256]{3,2,0,1:T(8,128)(2,1)}), bf16[64,8,8,256]{3,2,0,1:T(8,128)(2,1)}, u32[]{:S(2)}, u32[]{:S(2)}) %all-to-all-start) | async-done | bytes 2097184 | tf_op jit(solution)/shard_map/all_to_all | solution.py:29
  141.8 0.0 copy-start.1
  141.8 2.2 %copy.22 = bf16[8,64,1,8,256]{4,1,0,3,2:T(8,128)(2,1)S(1)} copy(bf16[8,64,1,8,256]{4,3,1,0,2:T(8,128)(2,1)} %bitcast.3) | data formatting | bytes 4194304 | tf_op jit(solution)/shard_map/all_to_all | solution.py:29
  144.1 0.0 copy-done.1
  144.1 4.7 %fusion.3 = f32[8,512,512]{2,1,0:T(8,128)} fusion(bf16[512,8,256]{2,0,1:T(8,128)(2,1)S(1)} %bitcast.29, bf16[32,8,8,512]{3,2,1,0:T(8,128)(2,1)S(1)} %bitcast.31, bf16[8,512]{1,0:T(8,128)(2,1)S(1)} %fusion.6), kind=kOutput, calls=%fused_computation.6 | convolution fusion | flops 1074790400 | bytes 12591104 | tf_op jit(solution)/shard_map/rki,jkr->kij/dot_general | solution.py:35
  148.8 0.0 reduce-scatter.3.cloned.1.call-update
  148.8 0.0 reduce-scatter.5.cloned.1.call-done
  148.8 2.1 %convert_element_type.27 = bf16[64,32,64]{2,1,0:T(8,128)(2,1)} convert(f32[64,32,64]{2,1,0:T(8,128)} %reduce-scatter.5.cloned.1.call-done) | non-fusion elementwise | flops 131072 | bytes 786432 | tf_op jit(solution)/shard_map/convert_element_type | solution.py:32
  150.9 13.8 %reduce-scatter.3.cloned.1.call-done = f32[8,256,512]{2,1,0:T(8,128)} async-done(((f32[8,512,512]{2,1,0:T(8,128)}), f32[8,256,512]{2,1,0:T(8,128)}) %reduce-scatter.3.cloned.1.call-update) | async-done | bytes 4194320 | tf_op jit(solution)/shard_map/reduce_scatter | solution.py:36
  164.8 3.8 %convert_element_type.24 = bf16[8,256,512]{2,1,0:T(8,128)(2,1)} convert(f32[8,256,512]{2,1,0:T(8,128)} %reduce-scatter.3.cloned.1.call-done) | non-fusion elementwise | flops 1048576 | bytes 6291456 | tf_op jit(solution)/shard_map/convert_element_type | solution.py:36
Async XLA Ops:
  7.2 0.8 copy-start.3
  7.2 18.8 %copy-start = (bf16[256,4096]{1,0:T(8,128)(2,1)S(1)}, bf16[256,4096]{1,0:T(8,128)(2,1)}, u32[]{:S(2)}) copy-start(bf16[256,4096]{1,0:T(8,128)(2,1)} %param.5) | copy-start | bytes 6291460
  7.2 18.8 %all-gather.2.cloned.1.call-start = ((), (), s32[]{:S(2)}) async-start(), calls=%async_computation.5 | async-start | bytes 6291456 | tf_op jit(solution)/shard_map/all_gather | solution.py:16
  35.1 54.6 %all-to-all-start.1 = ((bf16[8,8,64,256]{3,2,0,1:T(8,128)(2,1)}), bf16[8,8,64,256]{3,2,0,1:T(8,128)(2,1)}, u32[]{:S(2)}, u32[]{:S(2)}) async-start(bf16[8,8,64,256]{3,2,0,1:T(8,128)(2,1)} %copy.25), calls=%async_computation.2 | async-start | bytes 4194304 | tf_op jit(solution)/shard_map/all_to_all | solution.py:21
  40.8 3.3 %copy-start.2 = (bf16[64,32,64]{2,1,0:T(8,128)(2,1)S(1)}, bf16[64,32,64]{2,1,0:T(8,128)(2,1)}, u32[]{:S(2)}) copy-start(bf16[64,32,64]{2,1,0:T(8,128)(2,1)} %param.8) | copy-start | bytes 786436
  89.6 52.2 %all-to-all-start = ((bf16[64,8,8,256]{3,2,0,1:T(8,128)(2,1)}), bf16[64,8,8,256]{3,2,0,1:T(8,128)(2,1)}, u32[]{:S(2)}, u32[]{:S(2)}) async-start(bf16[64,8,8,256]{3,2,0,1:T(8,128)(2,1)} %copy.21), calls=%async_computation | async-start | bytes 4194304 | tf_op jit(solution)/shard_map/all_to_all | solution.py:29
  94.0 54.8 %reduce-scatter.5.cloned.1.call-start = ((), (), s32[]{:S(2)}) async-start(), calls=%async_computation.6 | async-start | bytes 3145728 | tf_op jit(solution)/shard_map/reduce_scatter | solution.py:32
  98.4 66.4 %reduce-scatter.3.cloned.1.call-start = ((), (), s32[]{:S(2)}) async-start(), calls=%async_computation.4 | async-start | bytes 12582912 | tf_op jit(solution)/shard_map/reduce_scatter | solution.py:36
  141.8 2.2 %copy-start.1 = (bf16[256,4096]{1,0:T(8,128)(2,1)S(1)}, bf16[256,4096]{1,0:T(8,128)(2,1)}, u32[]{:S(2)}) copy-start(bf16[256,4096]{1,0:T(8,128)(2,1)} %param.5) | copy-start | bytes 6291460
Sparse Core Ops, SparseCore 0:
  9.6 16.3 all-gather.1
  98.5 10.8 reduce-scatter.4
  148.9 15.8 reduce-scatter.2
where the time goes:
time: 176 us; the launch traced here: 175 us
  waiting for transfers between devices  117 us (66%)
  matrix products  14.4 us (8%)
  between operations  13.8 us (8%)
  local copies, waits for them, and re-layouts  11.3 us (6%)
  starting transfers between devices  10.2 us (6%)
  other arithmetic  5.95 us (3%)
  blocking collectives  2.56 us (1%)
    all_to_all x1, waiting for transfers between devices, on_device(): lax.all_to_all(back_sent, 'blk', split_axis=1, concat_axis=0, tiled=True)  43.4 us
    all_to_all x1, waiting for transfers between devices, on_device(): lax.all_to_all(mixed_sent, 'blk', split_axis=1, concat_axis=0, tiled=True)  40.7 us
    all_gather x1, waiting for transfers between devices, on_device(): left_full = lax.all_gather(left_factor, 'bin', axis=1, tiled=True)  18 us
    reduce_scatter x1, waiting for transfers between devices, on_device(): lax.psum_scatter(left_term, 'bin', scatter_dimension=1, tiled=True)  13.8 us
    all_to_all x1, starting transfers between devices, on_device(): lax.all_to_all(mixed_sent, 'blk', split_axis=1, concat_axis=0, tiled=True)  5.77 us
    dot_general x1, matrix products, on_device(): jnp.einsum('rki,kij->kjr', inputs, left_full, preferred_element_type=jnp....  4.76 us
    dot_general x1, matrix products, on_device(): jnp.einsum('rki,jkr->kij', inputs, returned, preferred_element_type=jnp.f...  4.66 us
    all_to_all x1, starting transfers between devices, on_device(): lax.all_to_all(back_sent, 'blk', split_axis=1, concat_axis=0, tiled=True)  4.36 us
  transfers between devices with their start and end apart: 5, of which 4 were waited for; matrix products, arithmetic and copies ran while one was open for 11% of the time, Pallas kernels for 0%

commit v1 on v0

--- a/solution.py
+++ b/solution.py
@@ -2,6 +2,29 @@
 import jax.numpy as jnp
 from jax import lax
 from jax.sharding import PartitionSpec as P
+
+
+def cut_along(x, dim, size):
+    before, after = (x.shape[:dim], x.shape[dim + 1 :])
+    return jnp.moveaxis(x.reshape(*before, size, -1, *after), dim, 0)
+
+
+def in_order(parts, dim):
+    parts = jnp.moveaxis(parts, 0, dim)
+    shape = parts.shape
+    return parts.reshape(*shape[:dim], shape[dim] * shape[dim + 1], *shape[dim + 2 :])
+
+
+def exchange_directly(array, axis, split_dim, concat_dim):
+    count, index = (lax.axis_size(axis), lax.axis_index(axis))
+    pieces = cut_along(array, split_dim, count)
+    whole = pieces
+    for turn in range(1, count):
+        target, source = ((index + turn) % count, (index - turn) % count)
+        sent = lax.dynamic_index_in_dim(pieces, target, 0)
+        partner_block = lax.ppermute(sent, axis, [(i, (i + turn) % count) for i in range(count)])
+        whole = lax.dynamic_update_slice_in_dim(whole, partner_block, source, axis=0)
+    return in_order(whole, concat_dim)
 
 
 def on_device(units, cotangent, left_factor, right_factor, session_units):
@@ -18,7 +41,7 @@
         "rki,kij->kjr", inputs, left_full, preferred_element_type=jnp.float32
     ).astype(jnp.bfloat16)
     mixed_sent = mixed.reshape(local_blocks, peer_count, right_local, row_count)
-    mixed_got = lax.all_to_all(mixed_sent, "blk", split_axis=1, concat_axis=0, tiled=True)
+    mixed_got = exchange_directly(mixed_sent, "blk", 1, 0)
     permuted = mixed_got.reshape(order_right, right_local, row_count)
     upstream = cotangent.reshape(row_count, right_local, order_right)
     right_full = lax.all_gather(right_factor, "bin", axis=1, tiled=True)

time: 176 us -> 168 us (0.955)
  waiting for transfers between devices: 117 us -> 58.3 us
  starting transfers between devices: 10.2 us -> 53 us
  local copies, waits for them, and re-layouts: 11.3 us -> 20.5 us
    ppermute x0 -> x7, starting transfers between devices: none -> 45.5 us  [exchange_directly(): lax.ppermute(sent, axis, [(i, (i + turn) % count) for i in range(count)])]
    all_to_all x1, waiting for transfers between devices: 43.4 us -> 0.01 us  [on_device(): lax.all_to_all(back_sent, 'blk', split_axis=1, concat_axis=0, tiled=True)]
    all_to_all x1 -> x0, waiting for transfers between devices: 40.7 us -> none  [on_device(): lax.all_to_all(mixed_sent, 'blk', split_axis=1, concat_axis=0, tiled=True)]
    ppermute x0 -> x7, waiting for transfers between devices: none -> 29.2 us  [exchange_directly(): lax.ppermute(sent, axis, [(i, (i + turn) % count) for i in range(count)])]
    all_gather x1, waiting for transfers between devices: 18 us -> 2.36 us  [on_device(): left_full = lax.all_gather(left_factor, 'bin', axis=1, tiled=True)]
    reduce_scatter x1, waiting for transfers between devices: 0.02 us -> 7.77 us  [on_device(): lax.psum_scatter(right_term, 'bin', scatter_dimension=1, tiled=True)]
    dynamic_update_slice x0 -> x8, local copies, waits for them, and re-layouts: none -> 7.08 us  [exchange_directly(): lax.dynamic_update_slice_in_dim(whole, partner_block, source, axis=0)]
    all_to_all x1 -> x0, starting transfers between devices: 5.77 us -> none  [on_device(): lax.all_to_all(mixed_sent, 'blk', split_axis=1, concat_axis=0, tiled=True)]
  transfers between devices with their start and end apart: 5 -> 11, of which waited for: 4 -> 6; matrix products, arithmetic and copies ran while one was open for 11% -> 22% of each run, Pallas kernels for 0% -> 0%
where the time goes in v1:
time: 168 us
  waiting for transfers between devices  58.3 us (35%)
  starting transfers between devices  53 us (32%)
  local copies, waits for them, and re-layouts  20.5 us (12%)
  between operations  13.9 us (8%)
  matrix products  13.5 us (8%)
  other arithmetic  5.95 us (4%)
  blocking collectives  2.64 us (2%)
    ppermute x7, starting transfers between devices, exchange_directly(): lax.ppermute(sent, axis, [(i, (i + turn) % count) for i in range(count)])  45.5 us
    ppermute x7, waiting for transfers between devices, exchange_directly(): lax.ppermute(sent, axis, [(i, (i + turn) % count) for i in range(count)])  29.2 us
    reduce_scatter x1, waiting for transfers between devices, on_device(): lax.psum_scatter(left_term, 'bin', scatter_dimension=1, tiled=True)  18.3 us
    reduce_scatter x1, waiting for transfers between devices, on_device(): lax.psum_scatter(right_term, 'bin', scatter_dimension=1, tiled=True)  7.77 us
    all_to_all x1, starting transfers between devices, on_device(): lax.all_to_all(back_sent, 'blk', split_axis=1, concat_axis=0, tiled=True)  7.3 us
    dynamic_update_slice x8, local copies, waits for them, and re-layouts, exchange_directly(): lax.dynamic_update_slice_in_dim(whole, partner_block, source, axis=0)  7.08 us
    dot_general x1, matrix products, on_device(): jnp.einsum('rki,kij->kjr', inputs, left_full, preferred_element_type=jnp....  5.44 us
    dot_general x1, matrix products, on_device(): jnp.einsum('rki,jkr->kij', inputs, returned, preferred_element_type=jnp.f...  4.65 us
  transfers between devices with their start and end apart: 11, of which 6 were waited for; matrix products, arithmetic and copies ran while one was open for 22% of the time, Pallas kernels for 0%

profile of v1, /device:TPU:0, one launch (start us, length us, event | category | flops | bytes accessed | tf_op | source)
XLA Modules:
  0.0 167.9 jit_solution(15973174507466853445)
XLA Ops:
  7.2 0.0 all-gather.2.cloned.1.call-start
  7.2 0.7 all-gather.2.cloned.1.call-update
  7.9 0.0 copy-start.1
  7.9 3.3 %copy.26 = bf16[256,4096]{0,1:T(8,128)(2,1)S(1)} copy(bf16[256,4096]{1,0:T(8,128)(2,1)} %param.6) | data formatting | bytes 4194304 | tf_op args[1]
  11.3 2.6 %all_gather.6 = bf16[64,64,64]{2,1,0:T(8,128)(2,1)S(1)} all-gather(bf16[64,32,64]{2,1,0:T(8,128)(2,1)S(1)} %copy-done.1), channel_id=1, replica_groups=mesh['grp'=2,'blk'=8,'bin'=2] {'bin'}, dimensions={1}, use_global_device_ids=true | all-gather | bytes 786432 | tf_op jit(solution)/shard_map/all_gather | solution.py:47
  13.9 0.7 convert_bitcast_fusion.1
  14.6 1.5 copy.27
  16.1 7.3 %all-to-all-start = ((bf16[64,8,8,256]{3,2,0,1:T(8,128)(2,1)}), bf16[64,8,8,256]{3,2,0,1:T(8,128)(2,1)}, u32[]{:S(2)}, u32[]{:S(2)}) async-start(bf16[64,8,8,256]{3,2,0,1:T(8,128)(2,1)} %copy.27), calls=%async_computation | async-start | bytes 4194304 | tf_op jit(solution)/shard_map/all_to_all | solution.py:52
  23.4 0.0 reduce-scatter.5.cloned.1.call-start
  23.5 0.1 fusion.5
  23.6 2.4 %all-gather.2.cloned.1.call-done = bf16[8,512,512]{2,1,0:T(8,128)(2,1)} async-done(((bf16[8,256,512]{2,1,0:T(8,128)(2,1)}), bf16[8,512,512]{2,1,0:T(8,128)(2,1)}) %all-gather.2.cloned.1.call-update) | async-done | bytes 4194320 | tf_op jit(solution)/shard_map/all_gather | solution.py:39
  25.9 5.4 %convert_bitcast_fusion = bf16[8,512,256]{1,2,0:T(8,128)(2,1)} fusion(bf16[8,512,512]{2,1,0:T(8,128)(2,1)} %all-gather.2.cloned.1.call-done, bf16[32,8,8,512]{3,2,1,0:T(8,128)(2,1)} %bitcast.43, bf16[8,512]{1,0:T(8,128)(2,1)S(1)} %fusion.5), kind=kOutput, calls=%fused_computation.3 | convolution fusion | flops 1075838976 | bytes 8396800 | tf_op jit(solution)/shard_map/rki,kij->kjr/dot_general | solution.py:40
  31.4 3.9 %copy.30 = bf16[8,512,256]{2,1,0:T(8,128)(2,1)} copy(bf16[8,512,256]{1,2,0:T(8,128)(2,1)} %convert_bitcast_fusion) | data formatting | bytes 4194304 | tf_op jit(solution)/shard_map/convert_element_type | solution.py:42
  35.3 2.5 %dynamic-slice_bitcast_fusion = (bf16[1,8,1,64,256]{4,3,0,1,2:T(8,128)(2,1)S(1)}, bf16[1,8,1,64,256]{4,3,0,1,2:T(8,128)(2,1)S(1)}, bf16[1,8,1,64,256]{4,3,0,1,2:...) fusion(bf16[8,8,1,64,256]{4,3,1,0,2:T(8,128)(2,1)} %bitcast.39,, ...), kind=kLoop, calls=%fused_computation.8 | loop fusion | bytes 3670044 | tf_op jit(solution)/shard_map/jit(dynamic_index_in_dim)/dynamic_slice | solution.py:24
  37.8 1.7 %collective-permute-start = (bf16[1,8,1,64,256]{4,3,0,1,2:T(8,128)(2,1)}, bf16[1,8,1,64,256]{4,3,0,1,2:T(8,128)(2,1)S(1)}, u32[]{:S(2)}, u32[]{:S(2)}) collective-permute-start(bf16[1,8,1,64,256]{4,3,0,1,2:T(8,128)(2,1)} %get-tuple-element.8), channel_id=1, source_target_pairs={{0,2},{2,4},{4,6},{6,8},{8,10},{10,12},{12,14},{14,0},{1,3},{3,5},... | collective-permute-start | bytes 786440 | tf_op jit(solution)/shard_map/ppermute | solution.py:25
  39.6 1.5 collective-permute-start.1
  41.0 2.4 %collective-permute-start.2 = (bf16[1,8,1,64,256]{4,3,0,1,2:T(8,128)(2,1)}, bf16[1,8,1,64,256]{4,3,0,1,2:T(8,128)(2,1)S(1)}, u32[]{:S(2)}, u32[]{:S(2)}) collective-permute-start(bf16[1,8,1,64,256]{4,3,0,1,2:T(8,128)(2,1)} %get-tuple-element.6), channel_id=1, source_target_pairs={{0,6},{2,8},{4,10},{6,12},{8,14},{10,0},{12,2},{14,4},{1,7},{3,9},... | collective-permute-start | bytes 786440 | tf_op jit(solution)/shard_map/ppermute | solution.py:25
  43.4 2.3 %collective-permute-start.6 = (bf16[1,8,1,64,256]{4,3,0,1,2:T(8,128)(2,1)S(1)}, bf16[1,8,1,64,256]{4,3,0,1,2:T(8,128)(2,1)S(1)}, u32[]{:S(2)}, u32[]{:S(2)}) collective-permute-start(bf16[1,8,1,64,256]{4,3,0,1,2:T(8,128)(2,1)S(1)} %get-tuple-element.2), channel_id=1, source_target_pairs={{0,14},{2,0},{4,2},{6,4},{8,6},{10,8},{12,10},{14,12},{1,15},{3,1}... | collective-permute-start | bytes 786440 | tf_op jit(solution)/shard_map/ppermute | solution.py:25
  45.8 0.5 collective-permute-start.5
  46.3 23.0 %collective-permute-done = bf16[1,8,1,64,256]{4,3,0,1,2:T(8,128)(2,1)S(1)} collective-permute-done((bf16[1,8,1,64,256]{4,3,0,1,2:T(8,128)(2,1)}, bf16[1,8,1,64,256]{4,3,0,1,2:T(8,128)(2,1)S(1)}, u32[]{:S(2)}, u32[]{:S(2)}) %collective-permute-start) | collective-permute-done | bytes 262176 | tf_op jit(solution)/shard_map/ppermute | solution.py:25
  69.3 32.2 %collective-permute-start.3 = (bf16[1,8,1,64,256]{4,3,0,1,2:T(8,128)(2,1)}, bf16[1,8,1,64,256]{4,3,0,1,2:T(8,128)(2,1)S(1)}, u32[]{:S(2)}, u32[]{:S(2)}) collective-permute-start(bf16[1,8,1,64,256]{4,3,0,1,2:T(8,128)(2,1)} %get-tuple-element.5), channel_id=1, source_target_pairs={{0,8},{2,10},{4,12},{6,14},{8,0},{10,2},{12,4},{14,6},{1,9},{3,11}... | collective-permute-start | bytes 786440 | tf_op jit(solution)/shard_map/ppermute | solution.py:25
  101.5 0.8 constant_dynamic-update-slice_fusion.6
  102.3 0.0 collective-permute-done.1
  102.3 4.8 %collective-permute-start.4 = (bf16[1,8,1,64,256]{4,3,0,1,2:T(8,128)(2,1)}, bf16[1,8,1,64,256]{4,3,0,1,2:T(8,128)(2,1)S(1)}, u32[]{:S(2)}, u32[]{:S(2)}) collective-permute-start(bf16[1,8,1,64,256]{4,3,0,1,2:T(8,128)(2,1)} %get-tuple-element.4), channel_id=1, source_target_pairs={{0,10},{2,12},{4,14},{6,0},{8,2},{10,4},{12,6},{14,8},{1,11},{3,13... | collective-permute-start | bytes 786440 | tf_op jit(solution)/shard_map/ppermute | solution.py:25
  107.2 0.8 constant_dynamic-update-slice_fusion.5
  107.9 0.0 collective-permute-done.2
  107.9 0.7 constant_dynamic-update-slice_fusion.4
  108.7 5.8 %collective-permute-done.3 = bf16[1,8,1,64,256]{4,3,0,1,2:T(8,128)(2,1)S(1)} collective-permute-done((bf16[1,8,1,64,256]{4,3,0,1,2:T(8,128)(2,1)}, bf16[1,8,1,64,256]{4,3,0,1,2:T(8,128)(2,1)S(1)}, u32[]{:S(2)}, u32[]{:S(2)}) %collective-permute-start.3) | collective-permute-done | bytes 262176 | tf_op jit(solution)/shard_map/ppermute | solution.py:25
  114.5 0.7 constant_dynamic-update-slice_fusion.3
  115.2 0.3 collective-permute-done.4
  115.6 0.7 constant_dynamic-update-slice_fusion.2
  116.3 0.0 collective-permute-done.5
  116.3 0.8 constant_dynamic-update-slice_fusion.1
  117.1 0.0 collective-permute-done.6
  117.1 0.7 constant_dynamic-update-slice_fusion
  117.8 1.8 %copy.31 = bf16[8,8,1,64,256]{4,3,1,0,2:T(8,128)(2,1)S(1)} copy(bf16[8,8,1,64,256]{4,3,0,1,2:T(8,128)(2,1)} %constant_dynamic-update-slice_fusion) | data formatting | bytes 4194304 | tf_op jit(solution)/shard_map/dynamic_update_slice | solution.py:26
  119.6 2.8 %fusion = f32[64,64,64]{2,1,0:T(8,128)} fusion(bf16[256,64,64]{0,2,1:T(8,128)(2,1)S(1)} %bitcast.38, bf16[64,64,256]{2,1,0:T(8,128)(2,1)S(1)} %bitcast.41), kind=kOutput, calls=%fused_computation.1 | convolution fusion | flops 134217728 | bytes 5242880 | tf_op jit(solution)/shard_map/kjr,rjm->jkm/dot_general | solution.py:54
  122.4 0.0 reduce-scatter.5.cloned.1.call-update
  122.4 0.0 reduce-scatter.3.cloned.1.call-start
  122.5 0.0 all-to-all-done
  122.5 0.0 copy-start
  122.5 2.2 %copy.28 = bf16[8,64,1,8,256]{4,1,0,3,2:T(8,128)(2,1)S(1)} copy(bf16[8,64,1,8,256]{4,3,1,0,2:T(8,128)(2,1)} %bitcast.3) | data formatting | bytes 4194304 | tf_op jit(solution)/shard_map/all_to_all | solution.py:52
  124.7 4.6 %fusion.2 = f32[8,512,512]{2,1,0:T(8,128)} fusion(bf16[512,8,256]{2,0,1:T(8,128)(2,1)S(1)} %bitcast.42, bf16[32,8,8,512]{3,2,1,0:T(8,128)(2,1)S(1)} %bitcast.44, bf16[8,512]{1,0:T(8,128)(2,1)S(1)} %fusion.5), kind=kOutput, calls=%fused_computation.5 | convolution fusion | flops 1074790400 | bytes 12591104 | tf_op jit(solution)/shard_map/rki,jkr->kij/dot_general | solution.py:58
  129.4 0.0 reduce-scatter.3.cloned.1.call-update
  129.4 7.8 %reduce-scatter.5.cloned.1.call-done = f32[64,32,64]{2,1,0:T(8,128)} async-done(((f32[64,64,64]{2,1,0:T(8,128)}), f32[64,32,64]{2,1,0:T(8,128)}) %reduce-scatter.5.cloned.1.call-update) | async-done | bytes 524304 | tf_op jit(solution)/shard_map/reduce_scatter | solution.py:55
  137.2 2.1 %convert_element_type.27 = bf16[64,32,64]{2,1,0:T(8,128)(2,1)} convert(f32[64,32,64]{2,1,0:T(8,128)} %reduce-scatter.5.cloned.1.call-done) | non-fusion elementwise | flops 131072 | bytes 786432 | tf_op jit(solution)/shard_map/convert_element_type | solution.py:55
  139.3 18.3 %reduce-scatter.3.cloned.1.call-done = f32[8,256,512]{2,1,0:T(8,128)} async-done(((f32[8,512,512]{2,1,0:T(8,128)}), f32[8,256,512]{2,1,0:T(8,128)}) %reduce-scatter.3.cloned.1.call-update) | async-done | bytes 4194320 | tf_op jit(solution)/shard_map/reduce_scatter | solution.py:59
  157.6 3.8 %convert_element_type.24 = bf16[8,256,512]{2,1,0:T(8,128)(2,1)} convert(f32[8,256,512]{2,1,0:T(8,128)} %reduce-scatter.3.cloned.1.call-done) | non-fusion elementwise | flops 1048576 | bytes 6291456 | tf_op jit(solution)/shard_map/convert_element_type | solution.py:59
  (4 shorter events, 0.0 us)
Async XLA Ops:
  7.2 18.8 %all-gather.2.cloned.1.call-start = ((), (), s32[]{:S(2)}) async-start(), calls=%async_computation.4 | async-start | bytes 6291456 | tf_op jit(solution)/shard_map/all_gather | solution.py:39
  7.9 3.4 %copy-start.1 = (bf16[64,32,64]{2,1,0:T(8,128)(2,1)S(1)}, bf16[64,32,64]{2,1,0:T(8,128)(2,1)}, u32[]{:S(2)}) copy-start(bf16[64,32,64]{2,1,0:T(8,128)(2,1)} %param.8) | copy-start | bytes 786436
  16.1 7.5 %copy-start.2 = (s32[8]{0:T(128)S(1)}, s32[8]{0:T(128)}, u32[]{:S(2)}) copy-start(s32[8]{0:T(128)} %param.9) | copy-start | bytes 100
  16.1 106.4 %all-to-all-start = ((bf16[64,8,8,256]{3,2,0,1:T(8,128)(2,1)}), bf16[64,8,8,256]{3,2,0,1:T(8,128)(2,1)}, u32[]{:S(2)}, u32[]{:S(2)}) async-start(bf16[64,8,8,256]{3,2,0,1:T(8,128)(2,1)} %copy.27), calls=%async_computation | async-start | bytes 4194304 | tf_op jit(solution)/shard_map/all_to_all | solution.py:52
  23.4 113.8 %reduce-scatter.5.cloned.1.call-start = ((), (), s32[]{:S(2)}) async-start(), calls=%async_computation.5 | async-start | bytes 3145728 | tf_op jit(solution)/shard_map/reduce_scatter | solution.py:55
  37.8 31.5 %collective-permute-start = (bf16[1,8,1,64,256]{4,3,0,1,2:T(8,128)(2,1)}, bf16[1,8,1,64,256]{4,3,0,1,2:T(8,128)(2,1)S(1)}, u32[]{:S(2)}, u32[]{:S(2)}) collective-permute-start(bf16[1,8,1,64,256]{4,3,0,1,2:T(8,128)(2,1)} %get-tuple-element.8), channel_id=1, source_target_pairs={{0,2},{2,4},{4,6},{6,8},{8,10},{10,12},{12,14},{14,0},{1,3},{3,5},... | collective-permute-start | bytes 786440 | tf_op jit(solution)/shard_map/ppermute | solution.py:25
  39.6 62.8 %collective-permute-start.1 = (bf16[1,8,1,64,256]{4,3,0,1,2:T(8,128)(2,1)}, bf16[1,8,1,64,256]{4,3,0,1,2:T(8,128)(2,1)S(1)}, u32[]{:S(2)}, u32[]{:S(2)}) collective-permute-start(bf16[1,8,1,64,256]{4,3,0,1,2:T(8,128)(2,1)} %get-tuple-element.7), channel_id=1, source_target_pairs={{0,4},{2,6},{4,8},{6,10},{8,12},{10,14},{12,0},{14,2},{1,5},{3,7},... | collective-permute-start | bytes 786440 | tf_op jit(solution)/shard_map/ppermute | solution.py:25
  41.0 66.9 %collective-permute-start.2 = (bf16[1,8,1,64,256]{4,3,0,1,2:T(8,128)(2,1)}, bf16[1,8,1,64,256]{4,3,0,1,2:T(8,128)(2,1)S(1)}, u32[]{:S(2)}, u32[]{:S(2)}) collective-permute-start(bf16[1,8,1,64,256]{4,3,0,1,2:T(8,128)(2,1)} %get-tuple-element.6), channel_id=1, source_target_pairs={{0,6},{2,8},{4,10},{6,12},{8,14},{10,0},{12,2},{14,4},{1,7},{3,9},... | collective-permute-start | bytes 786440 | tf_op jit(solution)/shard_map/ppermute | solution.py:25
  43.4 73.6 %collective-permute-start.6 = (bf16[1,8,1,64,256]{4,3,0,1,2:T(8,128)(2,1)S(1)}, bf16[1,8,1,64,256]{4,3,0,1,2:T(8,128)(2,1)S(1)}, u32[]{:S(2)}, u32[]{:S(2)}) collective-permute-start(bf16[1,8,1,64,256]{4,3,0,1,2:T(8,128)(2,1)S(1)} %get-tuple-element.2), channel_id=1, source_target_pairs={{0,14},{2,0},{4,2},{6,4},{8,6},{10,8},{12,10},{14,12},{1,15},{3,1}... | collective-permute-start | bytes 786440 | tf_op jit(solution)/shard_map/ppermute | solution.py:25
  45.8 70.5 %collective-permute-start.5 = (bf16[1,8,1,64,256]{4,3,0,1,2:T(8,128)(2,1)S(1)}, bf16[1,8,1,64,256]{4,3,0,1,2:T(8,128)(2,1)S(1)}, u32[]{:S(2)}, u32[]{:S(2)}) collective-permute-start(bf16[1,8,1,64,256]{4,3,0,1,2:T(8,128)(2,1)S(1)} %get-tuple-element.3), channel_id=1, source_target_pairs={{0,12},{2,14},{4,0},{6,2},{8,4},{10,6},{12,8},{14,10},{1,13},{3,15... | collective-permute-start | bytes 786440 | tf_op jit(solution)/shard_map/ppermute | solution.py:25
  69.3 45.2 %collective-permute-start.3 = (bf16[1,8,1,64,256]{4,3,0,1,2:T(8,128)(2,1)}, bf16[1,8,1,64,256]{4,3,0,1,2:T(8,128)(2,1)S(1)}, u32[]{:S(2)}, u32[]{:S(2)}) collective-permute-start(bf16[1,8,1,64,256]{4,3,0,1,2:T(8,128)(2,1)} %get-tuple-element.5), channel_id=1, source_target_pairs={{0,8},{2,10},{4,12},{6,14},{8,0},{10,2},{12,4},{14,6},{1,9},{3,11}... | collective-permute-start | bytes 786440 | tf_op jit(solution)/shard_map/ppermute | solution.py:25
  102.3 13.2 %collective-permute-start.4 = (bf16[1,8,1,64,256]{4,3,0,1,2:T(8,128)(2,1)}, bf16[1,8,1,64,256]{4,3,0,1,2:T(8,128)(2,1)S(1)}, u32[]{:S(2)}, u32[]{:S(2)}) collective-permute-start(bf16[1,8,1,64,256]{4,3,0,1,2:T(8,128)(2,1)} %get-tuple-element.4), channel_id=1, source_target_pairs={{0,10},{2,12},{4,14},{6,0},{8,2},{10,4},{12,6},{14,8},{1,11},{3,13... | collective-permute-start | bytes 786440 | tf_op jit(solution)/shard_map/ppermute | solution.py:25
  122.4 35.2 %reduce-scatter.3.cloned.1.call-start = ((), (), s32[]{:S(2)}) async-start(), calls=%async_computation.3 | async-start | bytes 12582912 | tf_op jit(solution)/shard_map/reduce_scatter | solution.py:59
  122.5 2.2 %copy-start = (bf16[256,4096]{1,0:T(8,128)(2,1)S(1)}, bf16[256,4096]{1,0:T(8,128)(2,1)}, u32[]{:S(2)}) copy-start(bf16[256,4096]{1,0:T(8,128)(2,1)} %param.5) | copy-start | bytes 6291460
Sparse Core Ops, SparseCore 0:
  9.5 16.3 all-gather.1
  122.5 14.5 reduce-scatter.4
  139.6 17.9 reduce-scatter.2
